TPU v7x, 32 devices: a whole 2x2x4 slice. The times are simulated.
32 devices in a mesh: grp: 2 (over y), wide: 4 (over z), col: 2 (over x), inc: 2 (over core).
Axes of the slice: x: 2, y: 2, z: 4, core: 2. Of those that a mesh axis runs over, the one named last changes fastest.
Arguments:
- values_in: bfloat16 [32, 64, 256, 512], P(('grp', 'col'), 'inc', 'wide'), parts along dimension 0, may hold values from -6 to 6
- shock_load: float32 [32], P(('grp', 'col')), parts along dimension 0, may hold values from -4 to 4
- price_field: float32 [128, 256, 512], P(('grp', 'inc'), 'wide'), parts along dimension 0, may hold values from -6 to 6
- rate_liquid: float32 [128, 256, 512], P(('grp', 'inc'), 'wide'), parts along dimension 0, may hold values from 0.05 to 0.5
- rate_illiquid: float32 [128, 256, 512], P(('grp', 'inc'), 'wide'), parts along dimension 0, may hold values from 0.05 to 0.5
- mask_liquid: int32 [128, 256, 512], P(('grp', 'inc'), 'wide'), parts along dimension 0, may hold values 0 or 1
- mask_illiquid: int32 [128, 256, 512], P(('grp', 'inc'), 'wide'), parts along dimension 0, may hold values 0 or 1
- jump_inverse: float32 [128, 64], P('grp'), parts along dimension 0, may hold values from -0.07 to 0.87
- coef_liquid: int32 [4096], replicated, may hold values from 0 to 127, as said below
- coef_illiquid: int32 [4096], replicated, may hold values from 0 to 255
- coef_income: int32 [4096], replicated, may hold values from 0 to 63
- owner: int32 [4096], replicated, may hold values from 0 to 7, as said below
Outputs:
- reduced: float32 [32, 8192], P(('grp', 'col'), ('wide', 'inc')), parts along dimension 0
There are 2 independent parts, one for each index of `grp`. A program takes and returns all parts, laid end to end along the dimension named above; an argument that names none is the same for every part. Nothing has to cross between parts.
Inputs may be any that keep to these rules, and one draw needn't show every extreme that they name: `coef_liquid`: every retained coefficient has liquid frequency below 128. No owner has more than 1024 rows, and some owner has exactly 1024.
All inputs are finite; a program needn't handle non-finite values. No bound on the sum of `mask_liquid` or of `mask_illiquid` on one device may be relied on, other than what follows from the above.
Results may differ from a plain program's by a relative error of at most 0.0003.
Values may be sent and summed in bfloat16 or wider, within the bound.
No kernel may reach another device: no remote copies, remote signals or barrier semaphores. Data moves between devices by JAX's collectives and lax.ppermute only.
A program may use at most 256 MiB of HBM per device.

v0:
```python
import jax
import jax.numpy as jnp
from jax import lax
from jax.sharding import PartitionSpec as P

NB = 512
NA = 256
NZ = 64
KBLOW = 128


def padded_2(cells, sides, width):
    for axis, dim in sides:
        count = lax.axis_size(axis)
        ends = count - 1
        head = lax.slice_in_dim(cells, 0, width, axis=dim)
        tail = lax.slice_in_dim(cells, cells.shape[dim] - width, cells.shape[dim], axis=dim)
        cells = jnp.concatenate(
            [
                lax.ppermute(tail, axis, [(i, (i + 1) % count) for i in range(ends)]),
                cells,
                lax.ppermute(head, axis, [((i + 1) % count, i) for i in range(ends)]),
            ],
            axis=dim,
        )
    return cells


def cosine_table(count):
    freq = jnp.arange(count, dtype=jnp.int32)[:, None]
    cell = jnp.arange(count, dtype=jnp.int32)[None, :]
    phase = (2 * cell + 1) * freq % (4 * count)
    angle = jnp.pi * phase.astype(jnp.float32) / (2.0 * count)
    first = jnp.where(freq == 0, jnp.sqrt(jnp.float32(0.5)), jnp.float32(1.0))
    return jnp.cos(angle) * jnp.sqrt(jnp.float32(2.0 / count)) * first


def slot_targets(owner, owners, capacity):
    onehot = (owner[:, None] == jnp.arange(owners, dtype=jnp.int32)[None, :]).astype(jnp.int32)
    before = jnp.cumsum(onehot, axis=0) - onehot
    slot = jnp.sum(before * onehot, axis=1)
    return owner * capacity + slot


def body(
    values_in,
    shock_load,
    price_field,
    rate_liquid,
    rate_illiquid,
    mask_liquid,
    mask_illiquid,
    jump_inverse,
    coef_liquid,
    coef_illiquid,
    coef_income,
    owner,
):
    high = lax.Precision.HIGH
    columns, nz_loc, na_loc, _ = values_in.shape
    wide_pos = lax.axis_index("wide")
    inc_pos = lax.axis_index("inc")
    wide_count = lax.axis_size("wide")
    padded = padded_2(values_in, (("wide", 2),), 1).astype(jnp.float32)
    center = padded[:, :, 1:-1]
    lower = jnp.where(wide_pos == 0, center[:, :, 0:1], padded[:, :, 0:1])
    upper = jnp.where(wide_pos == wide_count - 1, center[:, :, -1:], padded[:, :, -1:])
    fwd_a = jnp.concatenate([center[:, :, 1:], upper], axis=2) - center
    bwd_a = center - jnp.concatenate([lower, center[:, :, :-1]], axis=2)
    step_b = center[:, :, :, 1:] - center[:, :, :, :-1]
    zero_b = jnp.zeros(center.shape[:3] + (1,), jnp.float32)
    fwd_b = jnp.concatenate([step_b, zero_b], axis=3)
    bwd_b = jnp.concatenate([zero_b, step_b], axis=3)
    mask_b = mask_liquid.astype(jnp.float32)
    mask_a = mask_illiquid.astype(jnp.float32)
    load = shock_load[:, None, None, None]
    explicit = (
        center
        + rate_liquid * (mask_b * fwd_b - (1.0 - mask_b) * bwd_b)
        + rate_illiquid * (mask_a * fwd_a - (1.0 - mask_a) * bwd_a)
        + load * price_field
    )
    table_b = cosine_table(NB)[:KBLOW]
    liquid_part = jnp.einsum("kb,czab->czak", table_b, explicit, precision=high)
    table_a = lax.dynamic_slice_in_dim(cosine_table(NA), wide_pos * na_loc, na_loc, axis=1)
    illiquid_part = jnp.einsum("ja,czak->jkcz", table_a, liquid_part, precision=high)
    rows = illiquid_part.reshape(NA * KBLOW, columns * nz_loc)
    picked = jnp.take(rows, coef_illiquid * KBLOW + coef_liquid, axis=0)
    folded = jnp.dot(cosine_table(NZ), jump_inverse, precision=lax.Precision.HIGHEST)
    folded = lax.dynamic_slice_in_dim(folded, inc_pos * nz_loc, nz_loc, axis=1)
    weight = jnp.take(folded, coef_income, axis=0)
    partial = jnp.sum(picked.reshape(-1, columns, nz_loc) * weight[:, None, :], axis=2)
    kept = lax.psum(partial, ("wide", "inc"))
    owners = lax.axis_size(("wide", "inc"))
    count = owner.shape[0]
    capacity = 2 * count // owners
    targets = slot_targets(owner, owners, capacity)
    source = (
        jnp.full((owners * capacity,), count, jnp.int32)
        .at[targets]
        .set(jnp.arange(count, dtype=jnp.int32))
    )
    mine = lax.dynamic_slice_in_dim(source, lax.axis_index(("wide", "inc")) * capacity, capacity)
    gathered = jnp.take(kept, jnp.minimum(mine, count - 1), axis=0)
    return jnp.where((mine < count)[None, :], gathered.T, jnp.float32(0.0))


def solution(mesh):
    placed = (
        P(("grp", "col"), "inc", "wide", None),
        P(("grp", "col")),
        P(("grp", "inc"), "wide", None),
        P(("grp", "inc"), "wide", None),
        P(("grp", "inc"), "wide", None),
        P(("grp", "inc"), "wide", None),
        P(("grp", "inc"), "wide", None),
        P("grp", None),
        P(),
        P(),
        P(),
        P(),
    )
    return jax.shard_map(
        body,
        mesh=mesh,
        in_specs=placed,
        out_specs=P(("grp", "col"), ("wide", "inc")),
        check_vma=False,
    )
```

profile of v0, /device:TPU:0, one launch (start us, length us, event | category | flops | bytes accessed | tf_op | source)
XLA Modules:
  0.0 500.5 jit_solution(14844286475312916411)
XLA Ops:
  6.5 0.0 all-reduce.4.cloned.1.call-start
  6.6 3.3 fusion.94
  9.9 5.6 %collective-permute-start = (bf16[8,32,1,512]{3,1,2,0:T(8,128)(2,1)S(1)}, bf16[8,32,1,512]{3,1,2,0:T(8,128)(2,1)}, u32[]{:S(2)}, u32[]{:S(2)}) collective-permute-start(bf16[8,32,1,512]{3,1,2,0:T(8,128)(2,1)S(1)} %copy.34), channel_id=1, source_target_pairs={{0,4},{4,8},{8,12},{1,5},{5,9},{9,13},{2,6},{6,10},{10,14},{3,7},{... | collective-permute-start | bytes 786440 | tf_op jit(solution)/shard_map/ppermute | solution.py:20
  15.6 0.7 copy.35
  16.3 1.3 collective-permute-start.1
  17.6 4.9 convert_element_type.28
  22.6 8.5 %broadcast_subtract_fusion = (f32[32,64,512]{2,1,0:T(8,128)}, f32[32,64,512]{2,1,0:T(8,128)}) fusion(s32[32,64,512]{2,1,0:T(8,128)} %param.18, s32[32,64,512]{2,1,0:T(8,128)} %param.17), kind=kLoop, calls=%fused_computation.39 | loop fusion | flops 4194304 | bytes 16777216 | tf_op jit(solution)/shard_map/sub | solution.py:80
  31.1 4.9 convert_element_type.29
  36.0 0.8 broadcast_compare_fusion.3
  36.9 0.9 negate_select_fusion.2
  37.7 0.6 fusion.80
  38.4 0.6 broadcast_clamp_fusion
  39.0 0.6 compare_and_fusion.1
  39.6 0.3 negate_select_fusion
  39.8 0.3 fusion.60
  40.2 0.1 copy.28
  40.3 14.1 %gather_fusion.1 = f32[4096,32]{1,0:T(8,128)} fusion(f32[64,32]{1,0:T(8,128)S(1)} %copy.28, s32[4096]{0:T(1024)S(1)} %fusion.78), kind=kCustom, calls=%fused_computation.1 | custom fusion | bytes 1064960 | tf_op jit(solution)/shard_map/jit(_take)/gather | solution.py:91
  54.4 3.6 broadcast_select_fusion
  58.0 1.4 copy.29
  59.4 2.3 reduce-window.6
  61.7 0.3 slice_reduce_fusion
  62.0 0.2 reduce-window.9
  62.2 0.1 add_bitcast_fusion
  62.3 0.1 fusion.42
  62.5 15.5 %scatter_custom_fusion = s32[8192]{0:T(1024)S(1)} fusion(s32[4096]{0:T(1024)S(1)} %compare_select_fusion.2, s32[4096]{0:T(1024)S(1)} %iota.47, s32[]{:T(128)} %constant.66.clone.1), kind=kCustom, calls=%fused_computation.109 | custom fusion | bytes 32772 | tf_op jit(solution)/shard_map/scatter | solution.py:101
  78.1 0.6 fusion.79
  78.7 0.5 broadcast_compare_fusion.1
  79.2 1.4 copy.23
  80.6 1.4 copy.24
  82.0 20.9 %maximum_convert_fusion = f32[8,32,66,512]{3,2,1,0:T(8,128)} fusion(bf16[8,32,1,512]{3,2,1,0:T(2,128)(2,1)S(1)} %copy.24, bf16[8,32,64,512]{3,2,1,0:T(8,128)(2,1)} %param.12, bf16[8,32,1,512]{3,2,1,0:T(2,128)(2,1)S(1)} %copy.23), kind=kLoop, calls=%fused_computation.28 | loop fusion | flops 51904512 | bytes 51904512 | tf_op jit(solution)/shard_map/convert_element_type | solution.py:64
  102.9 47.7 %fusion.93 = (f32[8,32,63,512]{3,2,1,0:T(8,128)}, f32[8,32,63,512]{3,2,1,0:T(8,128)}) fusion(f32[8,32,66,512]{3,2,1,0:T(8,128)} %maximum_convert_fusion), kind=kLoop, calls=%fused_computation.140 | loop fusion | bytes 132120576 | tf_op jit(solution)/shard_map/slice | solution.py:69
  150.6 36.7 %slice_subtract_fusion = f32[8,32,64,511]{3,2,1,0:T(8,128)} fusion(f32[8,32,66,512]{3,2,1,0:T(8,128)} %maximum_convert_fusion), kind=kLoop, calls=%fused_computation.5 | loop fusion | flops 8372224 | bytes 100466688 | tf_op jit(solution)/shard_map/sub | solution.py:70
  187.3 4.8 broadcast_select_fusion.1
  192.2 73.0 %fusion.5 = f32[8,32,64,128]{3,2,1,0:T(8,128)} fusion(f32[8,32,1,512]{3,2,1,0:T(1,128)S(1)} %get-tuple-element.8, f32[8,32,63,512]{3,2,1,0:T(8,128)} %get-tuple-element.6, f32[8,32,63,512]{3,2,1,0:T(8,128)} %get-tuple-element.5, f32[8,32,1,512]{3,2,1,0:T(1,128)S(1)} %get-tuple-element.7, f32[8,32,66,512]{3,2,1,0:T(8,128)} %maximum_convert_fusion, ...), kind=kOutput, calls=%fused_computation.12 | convolution fusion | flops 6577061888 | bytes 173409280 | tf_op jit(solution)/shard_map/kb,czab->czak/dot_general | solution.py:84
  265.2 22.0 %convolution_bitcast_fusion = f32[256,128,8,32]{0,1,3,2:T(8,128)} fusion(f32[8,32,64,128]{3,2,1,0:T(8,128)} %fusion.5, s32[256,256]{0,1:T(8,128)} %negate_select_fusion.2, s32[]{:T(128)S(6)} %select_n.124, pred[256,256]{0,1:T(32,128)(4,1)} %get-tuple-element.16, pred[256,256]{0,1:T(32,128)(4,1)} %get-tuple-element.15, f32[256]{0:T(256)S(1)} %copy-done.14), kind=kOutput, calls=%fused_computation.37 | convolution fusion | flops 3221323776 | bytes 42042372 | tf_op jit(solution)/shard_map/ja,czak->jkcz/dot_general | solution.py:86
  287.3 31.1 %copy.25 = f32[256,128,8,32]{1,0,3,2:T(8,128)} copy(f32[256,128,8,32]{0,1,3,2:T(8,128)} %convolution_bitcast_fusion) | data formatting | bytes 67108864 | tf_op jit(solution)/shard_map/ja,czak->jkcz/transpose | solution.py:86
  318.4 31.8 %copy.40 = f32[32,8,256,128]{3,1,2,0:T(8,128)} copy(f32[32,8,256,128]{3,2,1,0:T(8,128)} %bitcast.48) | data formatting | bytes 67108864
  350.1 33.4 %copy.26 = f32[32768,256]{1,0:T(8,128)} copy(f32[32768,256]{0,1:T(8,128)} %bitcast.49) | data formatting | bytes 67108864 | tf_op jit(solution)/shard_map/reshape | solution.py:87
  383.6 26.7 %gather_fusion = f32[4096,256]{1,0:T(8,128)} fusion(f32[32768,256]{1,0:T(8,128)} %copy.26, s32[4096]{0:T(1024)S(1)} %copy-done.5), kind=kCustom, calls=%fused_computation | custom fusion | bytes 8404992 | tf_op jit(solution)/shard_map/jit(_take)/gather | solution.py:88
  410.3 5.6 %copy.27 = f32[4096,256]{0,1:T(8,128)} copy(f32[4096,256]{1,0:T(8,128)} %gather_fusion) | data formatting | bytes 8388608 | tf_op jit(solution)/shard_map/jit(_take)/gather | solution.py:88
  415.9 2.9 multiply_reduce_fusion
  418.8 1.9 copy.30
  420.7 0.0 all-reduce.4.cloned.1.call-update
  420.8 0.7 dynamic-slice_compare_fusion
  421.5 66.6 %all-reduce.4.cloned.1.call-done = f32[4096,8]{1,0:T(8,128)} async-done(((f32[4096,8]{1,0:T(8,128)}), f32[4096,8]{1,0:T(8,128)}) %all-reduce.4.cloned.1.call-update) | async-done | bytes 131088 | tf_op jit(solution)/shard_map/psum | solution.py:93
  488.1 4.4 gather_fusion.2
  492.5 0.3 select_bitcast_fusion
  492.8 0.8 copy.31
  (46 shorter events, 0.2 us)
Async XLA Ops:
  6.5 33.3 %copy-start = (f32[64,64]{1,0:T(8,128)S(1)}, f32[64,64]{1,0:T(8,128)}, u32[]{:S(2)}) copy-start(f32[64,64]{1,0:T(8,128)} %param.19) | copy-start | bytes 49156
  6.5 31.8 %copy-start.8 = (s32[4096]{0:T(1024)S(1)}, s32[4096]{0:T(1024)}, u32[]{:S(2)}) copy-start(s32[4096]{0:T(1024)} %param.22) | copy-start | bytes 49156
  6.5 31.8 %copy-start.6 = (s32[4096]{0:T(1024)S(1)}, s32[4096]{0:T(1024)}, u32[]{:S(2)}) copy-start(s32[4096]{0:T(1024)} %param.20) | copy-start | bytes 49156
  6.5 31.8 %copy-start.7 = (s32[4096]{0:T(1024)S(1)}, s32[4096]{0:T(1024)}, u32[]{:S(2)}) copy-start(s32[4096]{0:T(1024)} %param.21) | copy-start | bytes 49156
  6.5 52.9 %copy-start.4 = (s32[4096]{0:T(1024)S(1)}, s32[4096]{0:T(1024)}, u32[]{:S(2)}) copy-start(s32[4096]{0:T(1024)} %param.23) | copy-start | bytes 49156
  6.5 481.5 %all-reduce.4.cloned.1.call-start = ((), (), s32[]{:S(2)}) async-start(), calls=%async_computation | async-start | bytes 4194304 | tf_op jit(solution)/shard_map/psum | solution.py:93
  9.9 69.3 %collective-permute-start = (bf16[8,32,1,512]{3,1,2,0:T(8,128)(2,1)S(1)}, bf16[8,32,1,512]{3,1,2,0:T(8,128)(2,1)}, u32[]{:S(2)}, u32[]{:S(2)}) collective-permute-start(bf16[8,32,1,512]{3,1,2,0:T(8,128)(2,1)S(1)} %copy.34), channel_id=1, source_target_pairs={{0,4},{4,8},{8,12},{1,5},{5,9},{9,13},{2,6},{6,10},{10,14},{3,7},{... | collective-permute-start | bytes 786440 | tf_op jit(solution)/shard_map/ppermute | solution.py:20
  16.3 64.3 %collective-permute-start.1 = (bf16[8,32,1,512]{3,1,2,0:T(8,128)(2,1)}, bf16[8,32,1,512]{3,1,2,0:T(8,128)(2,1)}, u32[]{:S(2)}, u32[]{:S(2)}) collective-permute-start(bf16[8,32,1,512]{3,1,2,0:T(8,128)(2,1)} %copy.35), channel_id=1, source_target_pairs={{4,0},{8,4},{12,8},{5,1},{9,5},{13,9},{6,2},{10,6},{14,10},{7,3},{... | collective-permute-start | bytes 786440 | tf_op jit(solution)/shard_map/ppermute | solution.py:22
  36.0 66.9 %copy-start.13 = (f32[512]{0:T(512)}, f32[512]{0:T(512)S(1)}, u32[]{:S(2)}) copy-start(f32[512]{0:T(512)S(1)} %select_multiply_fusion) | copy-start | bytes 6148
  78.0 72.6 %copy-start.9 = (s32[8192]{0:T(1024)}, s32[8192]{0:T(1024)S(1)}, u32[]{:S(2)}) copy-start(s32[8192]{0:T(1024)S(1)} %scatter_custom_fusion) | copy-start | bytes 98308
  150.6 41.6 %copy-start.10 = (f32[8]{0:T(128)S(1)}, f32[8]{0:T(128)}, u32[]{:S(2)}) copy-start(f32[8]{0:T(128)} %param.13) | copy-start | bytes 100
  150.6 41.6 %slice-start = ((f32[512]{0:T(512)}), f32[128]{0:T(128)S(1)}, s32[]{:S(2)}) async-start(f32[512]{0:T(512)} %copy-done.13), calls=%async_computation.1 | async-start | bytes 1024 | tf_op jit(solution)/shard_map/slice | solution.py:83
  187.3 4.9 copy-start.2
  192.2 73.0 %copy-start.14 = (f32[256]{0:T(256)S(1)}, f32[256]{0:T(256)}, u32[]{:S(2)}) copy-start(f32[256]{0:T(256)} %fusion.80) | copy-start | bytes 3076
  350.1 33.4 %copy-start.5 = (s32[4096]{0:T(1024)S(1)}, s32[4096]{0:T(1024)}, u32[]{:S(2)}) copy-start(s32[4096]{0:T(1024)} %broadcast_clamp_fusion) | copy-start | bytes 49156
  350.1 143.5 %copy-start.1 = (f32[64,64]{1,0:T(8,128)S(1)}, f32[64,64]{1,0:T(8,128)}, u32[]{:S(2)}) copy-start(f32[64,64]{1,0:T(8,128)} %param.19) | copy-start | bytes 49156
  383.6 32.3 %copy-start.3 = (f32[4096,32]{0,1:T(8,128)S(1)}, f32[4096,32]{0,1:T(8,128)}, u32[]{:S(2)}) copy-start(f32[4096,32]{0,1:T(8,128)} %copy.29) | copy-start | bytes 1572868
  383.6 32.3 %copy-start.11 = (pred[4096]{0:T(1024)(128)(4,1)S(1)}, pred[4096]{0:T(1024)(128)(4,1)}, u32[]{:S(2)}) copy-start(pred[4096]{0:T(1024)(128)(4,1)} %compare_and_fusion.1) | copy-start | bytes 12292
  383.6 104.5 %copy-start.12 = (s32[1024]{0:T(1024)S(1)}, s32[1024]{0:T(1024)}, u32[]{:S(2)}) copy-start(s32[1024]{0:T(1024)} %fusion.79) | copy-start | bytes 12292
Sparse Core Ops, SparseCore 0:
  420.9 67.1 all-reduce.3
where the time goes:
time: 502 us; the launch traced here: 500 us
  local copies, waits for them, and re-layouts  222 us (44%)
  other arithmetic  96.1 us (19%)
  matrix products  95.4 us (19%)
  waiting for transfers between devices  66.7 us (13%)
  between operations  13.7 us (3%)
  starting transfers between devices  6.96 us (1%)
    dot_general x1, matrix products, body(): liquid_part = jnp.einsum('kb,czab->czak', table_b, explicit, precision=high)  73 us
    psum x1, waiting for transfers between devices, body(): kept = lax.psum(partial, ('wide', 'inc'))  66.6 us
    slice x1, local copies, waits for them, and re-layouts, body(): bwd_a = center - jnp.concatenate([lower, center[:, :, :-1]], axis=2)  47.7 us
    sub x1, other arithmetic, body(): step_b = center[:, :, :, 1:] - center[:, :, :, :-1]  36.7 us
    reshape x1, local copies, waits for them, and re-layouts, body(): rows = illiquid_part.reshape(NA * KBLOW, columns * nz_loc)  33.4 us
    unnamed x33, local copies, waits for them, and re-layouts  32.6 us
    gather x2, local copies, waits for them, and re-layouts, body(): picked = jnp.take(rows, coef_illiquid * KBLOW + coef_liquid, axis=0)  32.3 us
    transpose x1, local copies, waits for them, and re-layouts, body(): jnp.einsum('ja,czak->jkcz', table_a, liquid_part, precision=high)  31.1 us
  transfers between devices with their start and end apart: 3, of which 1 were waited for; matrix products, arithmetic and copies ran while one was open for 13% of the time, Pallas kernels for 0%

commit v1 on v0

--- a/solution.py
+++ b/solution.py
@@ -2,11 +2,18 @@
 import jax.numpy as jnp
 from jax import lax
 from jax.sharding import PartitionSpec as P
+from jax.lax import psum
 
 NB = 512
 NA = 256
 NZ = 64
 KBLOW = 128
+
+
+def unite_page(m):
+    for b in ("inc", "wide"):
+        m = psum(m, b)
+    return m
 
 
 def padded_2(cells, sides, width):
@@ -90,7 +97,7 @@
     folded = lax.dynamic_slice_in_dim(folded, inc_pos * nz_loc, nz_loc, axis=1)
     weight = jnp.take(folded, coef_income, axis=0)
     partial = jnp.sum(picked.reshape(-1, columns, nz_loc) * weight[:, None, :], axis=2)
-    kept = lax.psum(partial, ("wide", "inc"))
+    kept = unite_page(partial)
     owners = lax.axis_size(("wide", "inc"))
     count = owner.shape[0]
     capacity = 2 * count // owners

time: 502 us -> 531 us (1.058)
  waiting for transfers between devices: 66.7 us -> 98.2 us
    psum x1 -> x2, waiting for transfers between devices: 66.6 us -> 98.2 us  [unite_page(): m = psum(m, b)]
    unnamed x33 -> x35, local copies, waits for them, and re-layouts: 32.6 us -> 32.6 us
  transfers between devices with their start and end apart: 3 -> 4, of which waited for: 1 -> 2; matrix products, arithmetic and copies ran while one was open for 13% -> 12% of each run, Pallas kernels for 0% -> 0%
where the time goes in v1:
time: 531 us; the launch traced here: 529 us
  local copies, waits for them, and re-layouts  222 us (42%)
  waiting for transfers between devices  98.2 us (18%)
  matrix products  95.3 us (18%)
  other arithmetic  92.9 us (17%)
  between operations  13.7 us (3%)
  starting transfers between devices  6.99 us (1%)
    psum x2, waiting for transfers between devices, unite_page(): m = psum(m, b)  98.2 us
    dot_general x1, matrix products, body(): liquid_part = jnp.einsum('kb,czab->czak', table_b, explicit, precision=high)  73.2 us
    slice x1, local copies, waits for them, and re-layouts, body(): bwd_a = center - jnp.concatenate([lower, center[:, :, :-1]], axis=2)  47.7 us
    sub x1, other arithmetic, body(): step_b = center[:, :, :, 1:] - center[:, :, :, :-1]  36.7 us
    reshape x1, local copies, waits for them, and re-layouts, body(): rows = illiquid_part.reshape(NA * KBLOW, columns * nz_loc)  33.5 us
    unnamed x35, local copies, waits for them, and re-layouts  32.6 us
    gather x2, local copies, waits for them, and re-layouts, body(): picked = jnp.take(rows, coef_illiquid * KBLOW + coef_liquid, axis=0)  32.4 us
    transpose x1, local copies, waits for them, and re-layouts, body(): jnp.einsum('ja,czak->jkcz', table_a, liquid_part, precision=high)  31 us
  transfers between devices with their start and end apart: 4, of which 2 were waited for; matrix products, arithmetic and copies ran while one was open for 12% of the time, Pallas kernels for 0%

profile of v1, /device:TPU:0, one launch (start us, length us, event | category | flops | bytes accessed | tf_op | source)
XLA Modules:
  0.0 529.2 jit_solution(7804463718786950346)
XLA Ops:
  6.5 0.0 all-reduce.5.cloned.1.call-start
  6.6 3.4 fusion.94
  10.1 5.6 %collective-permute-start = (bf16[8,32,1,512]{3,1,2,0:T(8,128)(2,1)S(1)}, bf16[8,32,1,512]{3,1,2,0:T(8,128)(2,1)}, u32[]{:S(2)}, u32[]{:S(2)}) collective-permute-start(bf16[8,32,1,512]{3,1,2,0:T(8,128)(2,1)S(1)} %copy.34), channel_id=1, source_target_pairs={{0,4},{4,8},{8,12},{1,5},{5,9},{9,13},{2,6},{6,10},{10,14},{3,7},{... | collective-permute-start | bytes 786440 | tf_op jit(solution)/shard_map/ppermute | solution.py:27
  15.7 0.8 copy.35
  16.5 1.3 collective-permute-start.1
  17.8 4.9 convert_element_type.28
  22.7 8.5 %broadcast_subtract_fusion = (f32[32,64,512]{2,1,0:T(8,128)}, f32[32,64,512]{2,1,0:T(8,128)}) fusion(s32[32,64,512]{2,1,0:T(8,128)} %param.18, s32[32,64,512]{2,1,0:T(8,128)} %param.17), kind=kLoop, calls=%fused_computation.39 | loop fusion | flops 4194304 | bytes 16777216 | tf_op jit(solution)/shard_map/sub | solution.py:87
  31.2 2.5 convert_element_type.29
  33.7 0.9 broadcast_compare_fusion.3
  34.6 0.9 negate_select_fusion.2
  35.4 0.6 fusion.80
  36.1 0.6 broadcast_clamp_fusion
  36.7 0.6 compare_and_fusion.1
  37.3 0.3 negate_select_fusion
  37.6 0.3 fusion.60
  37.9 0.1 copy.28
  38.0 14.2 %gather_fusion.1 = f32[4096,32]{1,0:T(8,128)} fusion(f32[64,32]{1,0:T(8,128)S(1)} %copy.28, s32[4096]{0:T(1024)S(1)} %fusion.78), kind=kCustom, calls=%fused_computation.1 | custom fusion | bytes 1064960 | tf_op jit(solution)/shard_map/jit(_take)/gather | solution.py:98
  52.2 3.6 broadcast_select_fusion
  55.8 1.4 copy.29
  57.2 2.3 reduce-window.6
  59.6 0.3 slice_reduce_fusion
  59.9 0.2 reduce-window.9
  60.1 0.1 add_bitcast_fusion
  60.2 0.7 fusion.42
  60.9 0.5 broadcast_compare_fusion.1
  61.4 1.4 copy.23
  62.8 1.4 copy.24
  64.2 20.8 %maximum_convert_fusion = f32[8,32,66,512]{3,2,1,0:T(8,128)} fusion(bf16[8,32,1,512]{3,2,1,0:T(2,128)(2,1)S(1)} %copy.24, bf16[8,32,64,512]{3,2,1,0:T(8,128)(2,1)} %param.12, bf16[8,32,1,512]{3,2,1,0:T(2,128)(2,1)S(1)} %copy.23), kind=kLoop, calls=%fused_computation.28 | loop fusion | flops 51904512 | bytes 51904512 | tf_op jit(solution)/shard_map/convert_element_type | solution.py:71
  85.0 47.7 %fusion.93 = (f32[8,32,63,512]{3,2,1,0:T(8,128)}, f32[8,32,63,512]{3,2,1,0:T(8,128)}) fusion(f32[8,32,66,512]{3,2,1,0:T(8,128)} %maximum_convert_fusion), kind=kLoop, calls=%fused_computation.140 | loop fusion | bytes 132120576 | tf_op jit(solution)/shard_map/slice | solution.py:76
  132.7 36.7 %slice_subtract_fusion = f32[8,32,64,511]{3,2,1,0:T(8,128)} fusion(f32[8,32,66,512]{3,2,1,0:T(8,128)} %maximum_convert_fusion), kind=kLoop, calls=%fused_computation.5 | loop fusion | flops 8372224 | bytes 100466688 | tf_op jit(solution)/shard_map/sub | solution.py:77
  169.4 4.9 broadcast_select_fusion.1
  174.3 73.2 %fusion.5 = f32[8,32,64,128]{3,2,1,0:T(8,128)} fusion(f32[8,32,1,512]{3,2,1,0:T(1,128)S(1)} %get-tuple-element.8, f32[8,32,63,512]{3,2,1,0:T(8,128)} %get-tuple-element.6, f32[8,32,63,512]{3,2,1,0:T(8,128)} %get-tuple-element.5, f32[8,32,1,512]{3,2,1,0:T(1,128)S(1)} %get-tuple-element.7, f32[8,32,66,512]{3,2,1,0:T(8,128)} %maximum_convert_fusion, ...), kind=kOutput, calls=%fused_computation.12 | convolution fusion | flops 6577061888 | bytes 173409280 | tf_op jit(solution)/shard_map/kb,czab->czak/dot_general | solution.py:91
  247.5 21.8 %convolution_bitcast_fusion = f32[256,128,8,32]{0,1,3,2:T(8,128)} fusion(f32[8,32,64,128]{3,2,1,0:T(8,128)} %fusion.5, s32[256,256]{0,1:T(8,128)} %negate_select_fusion.2, s32[]{:T(128)S(6)} %select_n.124, pred[256,256]{0,1:T(32,128)(4,1)} %get-tuple-element.16, pred[256,256]{0,1:T(32,128)(4,1)} %get-tuple-element.15, f32[256]{0:T(256)S(1)} %copy-done.15), kind=kOutput, calls=%fused_computation.37 | convolution fusion | flops 3221323776 | bytes 42042372 | tf_op jit(solution)/shard_map/ja,czak->jkcz/dot_general | solution.py:93
  269.3 31.0 %copy.25 = f32[256,128,8,32]{1,0,3,2:T(8,128)} copy(f32[256,128,8,32]{0,1,3,2:T(8,128)} %convolution_bitcast_fusion) | data formatting | bytes 67108864 | tf_op jit(solution)/shard_map/ja,czak->jkcz/transpose | solution.py:93
  300.4 31.7 %copy.40 = f32[32,8,256,128]{3,1,2,0:T(8,128)} copy(f32[32,8,256,128]{3,2,1,0:T(8,128)} %bitcast.48) | data formatting | bytes 67108864
  332.1 33.5 %copy.26 = f32[32768,256]{1,0:T(8,128)} copy(f32[32768,256]{0,1:T(8,128)} %bitcast.49) | data formatting | bytes 67108864 | tf_op jit(solution)/shard_map/reshape | solution.py:94
  365.6 26.8 %gather_fusion = f32[4096,256]{1,0:T(8,128)} fusion(f32[32768,256]{1,0:T(8,128)} %copy.26, s32[4096]{0:T(1024)S(1)} %copy-done.7), kind=kCustom, calls=%fused_computation | custom fusion | bytes 8404992 | tf_op jit(solution)/shard_map/jit(_take)/gather | solution.py:95
  392.4 5.6 %copy.27 = f32[4096,256]{0,1:T(8,128)} copy(f32[4096,256]{1,0:T(8,128)} %gather_fusion) | data formatting | bytes 8388608 | tf_op jit(solution)/shard_map/jit(_take)/gather | solution.py:95
  398.0 2.9 multiply_reduce_fusion
  400.9 1.9 copy.30
  402.9 0.0 all-reduce.5.cloned.1.call-update
  402.9 0.0 all-reduce.7.cloned.1.call-start
  403.0 15.5 %scatter_custom_fusion = s32[8192]{0:T(1024)S(1)} fusion(s32[4096]{0:T(1024)S(1)} %compare_select_fusion.2, s32[4096]{0:T(1024)S(1)} %iota.47, s32[]{:T(128)} %constant.66.clone.1), kind=kCustom, calls=%fused_computation.109 | custom fusion | bytes 32772 | tf_op jit(solution)/shard_map/scatter | solution.py:108
  418.5 8.1 %all-reduce.5.cloned.1.call-done = f32[4096,8]{1,0:T(8,128)} async-done(((f32[4096,8]{1,0:T(8,128)}), f32[4096,8]{1,0:T(8,128)}) %all-reduce.5.cloned.1.call-update) | async-done | bytes 131088 | tf_op jit(solution)/shard_map/psum | solution.py:15
  426.7 90.1 %all-reduce.7.cloned.1.call-done = f32[4096,8]{1,0:T(8,128)} async-done(((f32[4096,8]{1,0:T(8,128)}), f32[4096,8]{1,0:T(8,128)}) %all-reduce.7.cloned.1.call-update) | async-done | bytes 131088 | tf_op jit(solution)/shard_map/psum | solution.py:15
  516.8 4.4 gather_fusion.2
  521.2 0.3 select_bitcast_fusion
  521.6 0.8 copy.31
  (51 shorter events, 0.2 us)
Async XLA Ops:
  6.5 31.0 %copy-start = (f32[64,64]{1,0:T(8,128)S(1)}, f32[64,64]{1,0:T(8,128)}, u32[]{:S(2)}) copy-start(f32[64,64]{1,0:T(8,128)} %param.19) | copy-start | bytes 49156
  6.5 29.5 %copy-start.11 = (s32[4096]{0:T(1024)S(1)}, s32[4096]{0:T(1024)}, u32[]{:S(2)}) copy-start(s32[4096]{0:T(1024)} %param.22) | copy-start | bytes 49156
  6.5 29.5 %copy-start.9 = (s32[4096]{0:T(1024)S(1)}, s32[4096]{0:T(1024)}, u32[]{:S(2)}) copy-start(s32[4096]{0:T(1024)} %param.20) | copy-start | bytes 49156
  6.5 29.6 %copy-start.10 = (s32[4096]{0:T(1024)S(1)}, s32[4096]{0:T(1024)}, u32[]{:S(2)}) copy-start(s32[4096]{0:T(1024)} %param.21) | copy-start | bytes 49156
  6.5 420.1 %all-reduce.5.cloned.1.call-start = ((), (), s32[]{:S(2)}) async-start(), calls=%async_computation | async-start | bytes 4194304 | tf_op jit(solution)/shard_map/psum | solution.py:15
  6.6 24.6 %copy-start.3 = (s32[32,64,512]{2,1,0:T(8,128)S(1)}, s32[32,64,512]{2,1,0:T(8,128)}, u32[]{:S(2)}) copy-start(s32[32,64,512]{2,1,0:T(8,128)} %param.18) | copy-start | bytes 12582916
  10.1 51.4 %collective-permute-start = (bf16[8,32,1,512]{3,1,2,0:T(8,128)(2,1)S(1)}, bf16[8,32,1,512]{3,1,2,0:T(8,128)(2,1)}, u32[]{:S(2)}, u32[]{:S(2)}) collective-permute-start(bf16[8,32,1,512]{3,1,2,0:T(8,128)(2,1)S(1)} %copy.34), channel_id=1, source_target_pairs={{0,4},{4,8},{8,12},{1,5},{5,9},{9,13},{2,6},{6,10},{10,14},{3,7},{... | collective-permute-start | bytes 786440 | tf_op jit(solution)/shard_map/ppermute | solution.py:27
  16.5 46.4 %collective-permute-start.1 = (bf16[8,32,1,512]{3,1,2,0:T(8,128)(2,1)}, bf16[8,32,1,512]{3,1,2,0:T(8,128)(2,1)}, u32[]{:S(2)}, u32[]{:S(2)}) collective-permute-start(bf16[8,32,1,512]{3,1,2,0:T(8,128)(2,1)} %copy.35), channel_id=1, source_target_pairs={{4,0},{8,4},{12,8},{5,1},{9,5},{13,9},{6,2},{10,6},{14,10},{7,3},{... | collective-permute-start | bytes 786440 | tf_op jit(solution)/shard_map/ppermute | solution.py:29
  31.2 26.0 %copy-start.5 = (s32[4096]{0:T(1024)S(1)}, s32[4096]{0:T(1024)}, u32[]{:S(2)}) copy-start(s32[4096]{0:T(1024)} %param.23) | copy-start | bytes 49156
  33.7 51.3 %copy-start.14 = (f32[512]{0:T(512)}, f32[512]{0:T(512)S(1)}, u32[]{:S(2)}) copy-start(f32[512]{0:T(512)S(1)} %select_multiply_fusion) | copy-start | bytes 6148
  169.4 4.9 copy-start.2
  169.4 4.9 copy-start.12
  169.4 4.9 slice-start
  174.3 73.2 %copy-start.15 = (f32[256]{0:T(256)S(1)}, f32[256]{0:T(256)}, u32[]{:S(2)}) copy-start(f32[256]{0:T(256)} %fusion.80) | copy-start | bytes 3076
  332.1 33.5 %copy-start.7 = (s32[4096]{0:T(1024)S(1)}, s32[4096]{0:T(1024)}, u32[]{:S(2)}) copy-start(s32[4096]{0:T(1024)} %broadcast_clamp_fusion) | copy-start | bytes 49156
  365.6 32.5 %copy-start.4 = (f32[4096,32]{0,1:T(8,128)S(1)}, f32[4096,32]{0,1:T(8,128)}, u32[]{:S(2)}) copy-start(f32[4096,32]{0,1:T(8,128)} %copy.29) | copy-start | bytes 1572868
  365.6 32.5 %copy-start.13 = (pred[4096]{0:T(1024)(128)(4,1)S(1)}, pred[4096]{0:T(1024)(128)(4,1)}, u32[]{:S(2)}) copy-start(pred[4096]{0:T(1024)(128)(4,1)} %compare_and_fusion.1) | copy-start | bytes 12292
  365.6 37.4 %copy-start.6 = (s32[4096]{0:T(1024)S(1)}, s32[4096]{0:T(1024)}, u32[]{:S(2)}) copy-start(s32[4096]{0:T(1024)} %param.23) | copy-start | bytes 49156
  365.6 37.4 %copy-start.8 = (s32[4096]{0:T(1024)S(1)}, s32[4096]{0:T(1024)}, u32[]{:S(2)}) copy-start(s32[4096]{0:T(1024)} %fusion.42) | copy-start | bytes 49156
  365.6 156.8 %copy-start.1 = (f32[64,64]{1,0:T(8,128)S(1)}, f32[64,64]{1,0:T(8,128)}, u32[]{:S(2)}) copy-start(f32[64,64]{1,0:T(8,128)} %param.19) | copy-start | bytes 49156
  402.9 113.9 %all-reduce.7.cloned.1.call-start = ((), (), s32[]{:S(2)}) async-start(), calls=%async_computation.1 | async-start | bytes 4194304 | tf_op jit(solution)/shard_map/psum | solution.py:15
Sparse Core Ops, SparseCore 0:
  403.0 23.5 all-reduce.4
  429.1 87.6 all-reduce.6
